TPU v7x, 256 devices: a whole 4x4x8 slice. The times are simulated.
256 devices in a mesh: cell: 16 (over z, core), energy: 16 (over y, x).
Axes of the slice: x: 4, y: 4, z: 8, core: 2. Of those that a mesh axis runs over, the one named last changes fastest.
Arguments:
- ham_diag: float32 [16, 768, 768], P('cell'), as said below
- couple: float32 [16, 128, 128], P('cell'), as said below
- couple_mask: int32 [16, 2, 2], P('cell'), may hold values from 0 to 1, as said below
- energies: float32 [16], P('energy'), may hold values from -0.02 to 0
- lead_front: float32 [16, 128, 128], P('energy'), as said below
- block_list: int32 [16, 16, 2], P('cell'), may hold values from 0 to 11, as said below
- derivative: float32 [16, 16, 4096], P('cell', 'energy'), may hold values from -0.24 to 0.24
- pair_list: int32 [16, 2], replicated, may hold values from 0 to 15
Outputs:
- local_density: float32 [16, 12288], P('energy', 'cell')
- phonon_self: float32 [16, 16, 16, 4096], P('cell', 'energy')
Inputs may be any that keep to these rules, and one draw needn't show every extreme that they name: Each block is symmetric with diagonal entries between 0.1 and 1.5. For every energy in the range of energies, the block-tridiagonal matrix with diagonal blocks ham_diag[c] - energy I and the masked couplings between cells, with coupled[0] lead_front[e] coupled[0]^T subtracted on the first 128 orbitals of cell 0, is positive definite, so that every shifted block, front and reduced matrix is positive definite. `couple`: with its own cell's couple_mask applied, each coupling has spectral norm at most 0.5. `lead_front`: each matrix is symmetric and positive definite with spectral norm at most 1.7, its diagonal entries in 0.5 to 1.5. `block_list`: entry 0 is the block row and entry 1 the block column of a listed 64-block of the cell; about half of the listed blocks are diagonal blocks. `couple_mask`: 1 keeps a block of the coupling, 0 removes it; the diagonal blocks of every cell are kept. `pair_list`: entry 0 names the energy of the first Green's function block, entry 1 that of the second.
All inputs are finite; a program needn't handle non-finite values.
Results may differ from a plain program's by a relative error of at most 0.0003.
Values sent between devices are 32-bit elements; how exact they have to be, the bound alone decides.
No kernel may reach another device: no remote copies, remote signals or barrier semaphores. Data moves between devices by JAX's collectives and lax.ppermute only.
A program may use at most 64 MiB of HBM per device.

v0:
```python
import jax
import jax.numpy as jnp
from jax import lax
from jax.sharding import PartitionSpec as P

BLK = 64


def passed_along(value, axis, steps):
    count = lax.axis_size(axis)
    first, last = (max(0, -steps), min(count, count - steps))
    return lax.ppermute(value, axis, [(source, source + steps) for source in range(first, last)])


def matmul(left_side, right_side):
    return jnp.matmul(left_side, right_side, precision=lax.Precision.HIGHEST)


def tmat(matrix):
    return jnp.swapaxes(matrix, -1, -2)


def invert_small(matrix):
    lower_factor = jnp.linalg.cholesky(matrix)
    identity = jnp.eye(matrix.shape[-1], dtype=matrix.dtype)
    lower_inverse = jax.scipy.linalg.solve_triangular(lower_factor, identity, lower=True)
    return matmul(lower_inverse.T, lower_inverse)


def sweep(matrix, span, pivot):
    column = matrix[:, span]
    scaled = matmul(column, pivot)
    matrix = matrix - matmul(scaled, column.T)
    scaled = scaled.at[span].set(-pivot)
    return matrix.at[:, span].set(scaled).at[span, :].set(scaled.T)


def lower_solve(lower_factor, rhs):
    return jax.scipy.linalg.solve_triangular(lower_factor, rhs, lower=True)


def expand_mask(couple, couple_mask):
    cell_count = couple.shape[0]
    mask_width = couple_mask.shape[1]
    shaped = couple.reshape(cell_count, mask_width, BLK, mask_width, BLK)
    return (shaped * couple_mask[:, :, None, :, None].astype(couple.dtype)).reshape(couple.shape)


def combine(left_seg, right_seg):
    p_a, q_a, r_a = left_seg
    p_b, q_b, r_b = right_seg
    surface = r_a.shape[-1]
    eye = jnp.eye(surface, dtype=r_a.dtype)
    root = jnp.linalg.cholesky(r_a)
    root_t = tmat(root)
    lp = matmul(root_t, p_b)
    reduced = eye - matmul(lp, root)
    root_reduced = jnp.linalg.cholesky(reduced)
    rhs = jnp.concatenate([matmul(root_t, q_b), matmul(lp, tmat(q_a))], axis=-1)
    solved = lower_solve(root_reduced, rhs)
    gram = matmul(tmat(solved), solved)
    r_c = r_b + gram[..., :surface, :surface]
    q_c = matmul(q_a, q_b) + gram[..., surface:, :surface]
    p_c = p_a + matmul(matmul(q_a, p_b), tmat(q_a)) + gram[..., surface:, surface:]
    return (p_c, q_c, r_c)


def self_energy(regrouped, derivative, pair_list):
    first_pick = jnp.take(regrouped, pair_list[:, 0], axis=0)
    second_pick = jnp.take(regrouped, pair_list[:, 1], axis=0)
    pair_count = pair_list.shape[0]
    listed = derivative.shape[0]
    first_pick = first_pick.reshape(pair_count, listed, BLK, BLK)
    second_pick = second_pick.reshape(pair_count, listed, BLK, BLK)
    coupling_mat = derivative.reshape(listed, BLK, BLK)
    high = lax.Precision.HIGHEST
    left_side = jnp.einsum("nij,pnjk->pnik", coupling_mat, first_pick, precision=high)
    left_side = jnp.einsum("pnik,nlk->pnil", left_side, coupling_mat, precision=high)
    result = jnp.einsum("pnil,pnml->npim", left_side, second_pick, precision=high)
    return result.reshape(listed, pair_count, BLK * BLK)


def on_device(
    ham_diag, couple, couple_mask, energies, lead_front, block_list, derivative, pair_list
):
    cell_count = lax.axis_size("cell")
    cell_index = lax.axis_index("cell")
    surface = couple.shape[1]
    size = ham_diag.shape[1]
    coupling = expand_mask(couple, couple_mask)[0]
    eye = jnp.eye(surface, dtype=jnp.float32)
    is_first = cell_index == 0
    is_last = cell_index == cell_count - 1

    lead_self = matmul(matmul(coupling, lead_front[0]), coupling.T)
    lead_self = jnp.where(is_first, lead_self, jnp.zeros_like(lead_self))
    shifted = ham_diag[0] - energies[0] * jnp.eye(size, dtype=jnp.float32)
    shifted = shifted.at[:surface, :surface].add(-lead_self)
    state = shifted
    for start in range(surface, size, surface):
        span = slice(start, start + surface)
        state = sweep(state, span, invert_small(state[span, span]))
    schur = state[:surface, :surface]
    schur_edge = state[:surface, -surface:]
    corner = invert_small(schur)
    leaf = (
        matmul(matmul(coupling.T, corner), coupling),
        -matmul(coupling.T, matmul(corner, schur_edge)),
        matmul(matmul(schur_edge.T, corner), schur_edge) - state[-surface:, -surface:],
    )
    prefix = leaf
    distance = 1
    while distance < cell_count:
        from_left = passed_along(prefix, "cell", distance)
        has_left = cell_index >= distance
        safe_left = (from_left[0], from_left[1], jnp.where(has_left, from_left[2], eye))
        joined = combine(safe_left, prefix)
        prefix = tuple(jnp.where(has_left, j, o) for j, o in zip(joined, prefix))
        distance *= 2

    front_before = passed_along(prefix[2], "cell", 1)
    left_self = matmul(matmul(coupling, front_before), coupling.T)
    left_self = jnp.where(is_first, jnp.zeros_like(left_self), left_self)
    first_span = slice(0, surface)
    green = -sweep(state, first_span, invert_small(schur - left_self))

    edge_rows = green[-surface:, :]
    step_b = matmul(coupling.T, green[:surface, -surface:])
    step_a = matmul(matmul(coupling.T, green[:surface, :surface]), coupling)
    distance = 1
    while distance < cell_count:
        far_a, far_b = passed_along((step_a, step_b), "cell", -distance)
        step_a = step_a + matmul(matmul(step_b, far_a), step_b.T)
        step_b = matmul(step_b, far_b)
        distance *= 2
    weights = passed_along(step_a, "cell", -1)
    weights = jnp.where(is_last, jnp.zeros_like(weights), weights)
    full = green + matmul(edge_rows.T, matmul(weights, edge_rows))

    local_density = jnp.diagonal(full)[None]
    block_count = size // BLK
    picked = full.reshape(block_count, BLK, block_count, BLK)[
        block_list[0, :, 0], :, block_list[0, :, 1], :
    ]
    picked = picked.reshape(1, block_list.shape[1], BLK * BLK)
    regrouped = lax.all_to_all(picked, "energy", split_axis=1, concat_axis=0, tiled=True)
    result = self_energy(regrouped, derivative[0], pair_list)
    return (local_density, result[None])


def solution(mesh):
    placed = (
        P("cell", None, None),
        P("cell", None, None),
        P("cell", None, None),
        P("energy"),
        P("energy", None, None),
        P("cell", None, None),
        P("cell", "energy", None),
        P(),
    )
    return jax.shard_map(
        on_device,
        mesh=mesh,
        in_specs=placed,
        out_specs=(P("energy", "cell"), P("cell", "energy", None, None)),
        check_vma=False,
    )
```

profile of v0, /device:TPU:97, one launch (start us, length us, event | category | flops | bytes accessed | tf_op | source)
XLA Modules:
  0.0 517.7 jit_solution(13109016660845739579)
XLA Ops:
  9.8 11.7 %cholesky.239 = f32[128,128]{1,0:T(8,128)S(1)} custom-call(f32[128,128]{1,0:T(8,128)S(1)} %fusion.103), custom_call_target="Cholesky" | custom-call | tf_op jit(solution)/shard_map/jit(cholesky)/cholesky | solution.py:24
  22.8 9.8 %custom-call.21 = f32[1,128,128]{1,2,0:T(8,128)S(1)} custom-call(f32[1,128,128]{2,1,0:T(8,128)S(1)} %fusion.57), custom_call_target="InvertDiagBlocksLowerTriangular" | custom-call | tf_op jit(solution)/shard_map/jit(_solve_triangular)/triangular_solve | solution.py:26
  35.0 3.9 convolution_subtract_fusion.5
  43.8 11.7 %cholesky.250 = f32[128,128]{1,0:T(8,128)S(1)} custom-call(f32[128,128]{1,0:T(8,128)S(1)} %fusion.101), custom_call_target="Cholesky" | custom-call | tf_op jit(solution)/shard_map/jit(cholesky)/cholesky | solution.py:24
  56.8 9.8 %custom-call.22 = f32[1,128,128]{1,2,0:T(8,128)S(1)} custom-call(f32[1,128,128]{2,1,0:T(8,128)S(1)} %fusion.58), custom_call_target="InvertDiagBlocksLowerTriangular" | custom-call | tf_op jit(solution)/shard_map/jit(_solve_triangular)/triangular_solve | solution.py:26
  69.0 3.9 convolution_subtract_fusion.4
  77.3 11.9 %cholesky.261 = f32[128,128]{1,0:T(8,128)S(1)} custom-call(f32[128,128]{1,0:T(8,128)S(1)} %fusion.99), custom_call_target="Cholesky" | custom-call | tf_op jit(solution)/shard_map/jit(cholesky)/cholesky | solution.py:24
  90.5 9.8 %custom-call.23 = f32[1,128,128]{1,2,0:T(8,128)S(1)} custom-call(f32[1,128,128]{2,1,0:T(8,128)S(1)} %fusion.59), custom_call_target="InvertDiagBlocksLowerTriangular" | custom-call | tf_op jit(solution)/shard_map/jit(_solve_triangular)/triangular_solve | solution.py:26
  109.7 11.7 %cholesky.272 = f32[128,128]{1,0:T(8,128)S(1)} custom-call(f32[128,128]{1,0:T(8,128)S(1)} %fusion.97), custom_call_target="Cholesky" | custom-call | tf_op jit(solution)/shard_map/jit(cholesky)/cholesky | solution.py:24
  122.8 10.0 %custom-call.24 = f32[1,128,128]{1,2,0:T(8,128)S(1)} custom-call(f32[1,128,128]{2,1,0:T(8,128)S(1)} %fusion.60), custom_call_target="InvertDiagBlocksLowerTriangular" | custom-call | tf_op jit(solution)/shard_map/jit(_solve_triangular)/triangular_solve | solution.py:26
  135.1 3.9 convolution_subtract_fusion.2
  143.4 11.7 %cholesky.283 = f32[128,128]{1,0:T(8,128)S(1)} custom-call(f32[128,128]{1,0:T(8,128)S(1)} %fusion.95), custom_call_target="Cholesky" | custom-call | tf_op jit(solution)/shard_map/jit(cholesky)/cholesky | solution.py:24
  156.5 9.8 %custom-call.25 = f32[1,128,128]{1,2,0:T(8,128)S(1)} custom-call(f32[1,128,128]{2,1,0:T(8,128)S(1)} %fusion.61), custom_call_target="InvertDiagBlocksLowerTriangular" | custom-call | tf_op jit(solution)/shard_map/jit(_solve_triangular)/triangular_solve | solution.py:26
  168.1 3.5 convolution_subtract_fusion.1
  175.2 11.7 %cholesky.294 = f32[128,128]{1,0:T(8,128)S(1)} custom-call(f32[128,128]{1,0:T(8,128)S(1)} %fusion.93), custom_call_target="Cholesky" | custom-call | tf_op jit(solution)/shard_map/jit(cholesky)/cholesky | solution.py:24
  188.2 9.8 %custom-call.26 = f32[1,128,128]{1,2,0:T(8,128)S(1)} custom-call(f32[1,128,128]{2,1,0:T(8,128)S(1)} %fusion.62), custom_call_target="InvertDiagBlocksLowerTriangular" | custom-call | tf_op jit(solution)/shard_map/jit(_solve_triangular)/triangular_solve | solution.py:26
  199.2 5.3 %collective-permute-start.3 = (f32[128,128]{0,1:T(8,128)S(1)}, f32[128,128]{0,1:T(8,128)S(1)}, u32[]{:S(2)}, u32[]{:S(2)}) collective-permute-start(f32[128,128]{0,1:T(8,128)S(1)} %copy.168), channel_id=1, source_target_pairs={{0,16},{16,32},{32,48},{48,64},{64,80},{80,96},{96,112},{112,128},... | collective-permute-start | bytes 196616 | tf_op jit(solution)/shard_map/ppermute | solution.py:12
  210.0 3.2 collective-permute-start.1
  213.4 11.7 %cholesky.305 = f32[128,128]{1,0:T(8,128)S(1)} custom-call(f32[128,128]{1,0:T(8,128)S(1)} %fusion.91), custom_call_target="Cholesky" | custom-call | tf_op jit(solution)/shard_map/jit(cholesky)/cholesky | solution.py:54
  228.6 11.7 %cholesky.316 = f32[128,128]{1,0:T(8,128)S(1)} custom-call(f32[128,128]{1,0:T(8,128)S(1)} %fusion.90), custom_call_target="Cholesky" | custom-call | tf_op jit(solution)/shard_map/jit(cholesky)/cholesky | solution.py:58
  241.7 9.8 %custom-call.27 = f32[1,128,128]{1,2,0:T(8,128)S(1)} custom-call(f32[1,128,128]{2,1,0:T(8,128)S(1)} %fusion.63), custom_call_target="InvertDiagBlocksLowerTriangular" | custom-call | tf_op jit(solution)/shard_map/jit(_solve_triangular)/triangular_solve | solution.py:39
  252.6 2.6 collective-permute-start.2
  255.4 2.7 collective-permute-start.4
  261.0 11.7 %cholesky.327 = f32[128,128]{1,0:T(8,128)S(1)} custom-call(f32[128,128]{1,0:T(8,128)S(1)} %fusion.88), custom_call_target="Cholesky" | custom-call | tf_op jit(solution)/shard_map/jit(cholesky)/cholesky | solution.py:54
  276.2 11.7 %cholesky.338 = f32[128,128]{1,0:T(8,128)S(1)} custom-call(f32[128,128]{1,0:T(8,128)S(1)} %fusion.87), custom_call_target="Cholesky" | custom-call | tf_op jit(solution)/shard_map/jit(cholesky)/cholesky | solution.py:58
  289.3 9.8 %custom-call.28 = f32[1,128,128]{1,2,0:T(8,128)S(1)} custom-call(f32[1,128,128]{2,1,0:T(8,128)S(1)} %fusion.64), custom_call_target="InvertDiagBlocksLowerTriangular" | custom-call | tf_op jit(solution)/shard_map/jit(_solve_triangular)/triangular_solve | solution.py:39
  304.9 2.3 collective-permute-start.9
  307.3 11.7 %cholesky.349 = f32[128,128]{1,0:T(8,128)S(1)} custom-call(f32[128,128]{1,0:T(8,128)S(1)} %fusion.85), custom_call_target="Cholesky" | custom-call | tf_op jit(solution)/shard_map/jit(cholesky)/cholesky | solution.py:54
  322.6 11.7 %cholesky.360 = f32[128,128]{1,0:T(8,128)S(1)} custom-call(f32[128,128]{1,0:T(8,128)S(1)} %fusion.84), custom_call_target="Cholesky" | custom-call | tf_op jit(solution)/shard_map/jit(cholesky)/cholesky | solution.py:58
  335.7 9.8 %custom-call.29 = f32[1,128,128]{1,2,0:T(8,128)S(1)} custom-call(f32[1,128,128]{2,1,0:T(8,128)S(1)} %fusion.65), custom_call_target="InvertDiagBlocksLowerTriangular" | custom-call | tf_op jit(solution)/shard_map/jit(_solve_triangular)/triangular_solve | solution.py:39
  350.3 11.7 %cholesky.371 = f32[128,128]{1,0:T(8,128)S(1)} custom-call(f32[128,128]{1,0:T(8,128)S(1)} %fusion.82), custom_call_target="Cholesky" | custom-call | tf_op jit(solution)/shard_map/jit(cholesky)/cholesky | solution.py:54
  365.5 11.7 %cholesky.382 = f32[128,128]{1,0:T(8,128)S(1)} custom-call(f32[128,128]{1,0:T(8,128)S(1)} %fusion.81), custom_call_target="Cholesky" | custom-call | tf_op jit(solution)/shard_map/jit(cholesky)/cholesky | solution.py:58
  378.6 9.8 %custom-call.30 = f32[1,128,128]{1,2,0:T(8,128)S(1)} custom-call(f32[1,128,128]{2,1,0:T(8,128)S(1)} %fusion.66), custom_call_target="InvertDiagBlocksLowerTriangular" | custom-call | tf_op jit(solution)/shard_map/jit(_solve_triangular)/triangular_solve | solution.py:39
  389.3 11.9 %collective-permute-start.11 = (f32[128,128]{0,1:T(8,128)S(1)}, f32[128,128]{0,1:T(8,128)S(1)}, u32[]{:S(2)}, u32[]{:S(2)}) collective-permute-start(f32[128,128]{0,1:T(8,128)S(1)} %fusion), channel_id=1, source_target_pairs={{0,16},{16,32},{32,48},{48,64},{64,80},{80,96},{96,112},{112,128},... | collective-permute-start | bytes 196616 | tf_op jit(solution)/shard_map/ppermute | solution.py:12
  403.8 11.7 %cholesky.393 = f32[128,128]{1,0:T(8,128)S(1)} custom-call(f32[128,128]{1,0:T(8,128)S(1)} %fusion.79), custom_call_target="Cholesky" | custom-call | tf_op jit(solution)/shard_map/jit(cholesky)/cholesky | solution.py:24
  416.8 9.8 %custom-call.31 = f32[1,128,128]{1,2,0:T(8,128)S(1)} custom-call(f32[1,128,128]{2,1,0:T(8,128)S(1)} %fusion.67), custom_call_target="InvertDiagBlocksLowerTriangular" | custom-call | tf_op jit(solution)/shard_map/jit(_solve_triangular)/triangular_solve | solution.py:26
  429.0 3.9 convolution_subtract_fusion
  441.5 3.2 collective-permute-done.12
  454.1 2.2 collective-permute-start.17
  456.3 4.1 collective-permute-done.16
  463.7 6.1 %collective-permute-done.18 = f32[128,128]{0,1:T(8,128)S(1)} collective-permute-done((f32[128,128]{0,1:T(8,128)S(1)}, f32[128,128]{0,1:T(8,128)S(1)}, u32[]{:S(2)}, u32[]{:S(2)}) %collective-permute-start.18) | collective-permute-done | bytes 65568 | tf_op jit(solution)/shard_map/ppermute | solution.py:12
  470.4 3.4 collective-permute-start.19
  478.7 3.9 convolution_add_fusion
  482.6 3.6 reshape.650
  486.2 6.2 %copy.205 = f32[12,64,12,64]{3,1,2,0:T(8,128)} copy(f32[12,64,12,64]{1,0,3,2:T(8,128)} %reshape.650) | data formatting | bytes 4718592 | tf_op jit(solution)/shard_map/reshape | solution.py:142
  492.4 2.9 gather_fusion.1
  496.4 6.8 %all-to-all-start = ((f32[1,16,4096]{2,0,1:T(1,128)}), f32[1,16,4096]{2,0,1:T(1,128)S(1)}, u32[]{:S(2)}, u32[]{:S(2)}) async-start(f32[1,16,4096]{2,0,1:T(1,128)} %reshape.651), calls=%async_computation | async-start | bytes 524288 | tf_op jit(solution)/shard_map/all_to_all | solution.py:146
  503.2 6.3 %gather_fusion = f32[768]{0:T(1024)S(1)} fusion(f32[768,768]{0,1:T(8,128)S(1)} %convolution_add_fusion, s32[768]{0:T(1024)S(1)} %or_reduce_fusion), kind=kCustom, calls=%fused_computation.2 | custom fusion | bytes 12288 | tf_op jit(solution)/shard_map/jit(diagonal)/cond/branch_0_fun/gather | solution.py:140
  (281 shorter events, 134.7 us)
Async XLA Ops:
  0.6 5.4 %copy-start = (f32[1,128,128]{2,1,0:T(8,128)S(1)}, f32[1,128,128]{2,1,0:T(8,128)}, u32[]{:S(2)}) copy-start(f32[1,128,128]{2,1,0:T(8,128)} %param.57) | copy-start | bytes 196612
  4.4 1.6 copy-start.4
  43.6 23.3 %copy-start.1 = (f32[768,768]{0,1:T(8,128)}, f32[768,768]{0,1:T(8,128)S(1)}, u32[]{:S(2)}) copy-start(f32[768,768]{0,1:T(8,128)S(1)} %bitcast_dynamic-update-slice_fusion.4) | copy-start | bytes 7077892
  103.8 1.4 copy-start.2
  199.2 59.2 %collective-permute-start.3 = (f32[128,128]{0,1:T(8,128)S(1)}, f32[128,128]{0,1:T(8,128)S(1)}, u32[]{:S(2)}, u32[]{:S(2)}) collective-permute-start(f32[128,128]{0,1:T(8,128)S(1)} %copy.168), channel_id=1, source_target_pairs={{0,16},{16,32},{32,48},{48,64},{64,80},{80,96},{96,112},{112,128},... | collective-permute-start | bytes 196616 | tf_op jit(solution)/shard_map/ppermute | solution.py:12
  206.7 6.6 %collective-permute-start = (f32[128,128]{0,1:T(8,128)S(1)}, f32[128,128]{0,1:T(8,128)S(1)}, u32[]{:S(2)}, u32[]{:S(2)}) collective-permute-start(f32[128,128]{0,1:T(8,128)S(1)} %convolution_subtract_fusion.10), channel_id=1, source_target_pairs={{0,16},{16,32},{32,48},{48,64},{64,80},{80,96},{96,112},{112,128},... | collective-permute-start | bytes 196616 | tf_op jit(solution)/shard_map/ppermute | solution.py:12
  210.0 41.5 %collective-permute-start.1 = (f32[128,128]{0,1:T(8,128)S(1)}, f32[128,128]{0,1:T(8,128)S(1)}, u32[]{:S(2)}, u32[]{:S(2)}) collective-permute-start(f32[128,128]{0,1:T(8,128)S(1)} %convolution_negate_fusion), channel_id=1, source_target_pairs={{0,16},{16,32},{32,48},{48,64},{64,80},{80,96},{96,112},{112,128},... | collective-permute-start | bytes 196616 | tf_op jit(solution)/shard_map/ppermute | solution.py:12
  252.6 8.3 %collective-permute-start.2 = (f32[128,128]{0,1:T(8,128)S(1)}, f32[128,128]{0,1:T(8,128)S(1)}, u32[]{:S(2)}, u32[]{:S(2)}) collective-permute-start(f32[128,128]{0,1:T(8,128)S(1)} %add_select_fusion.2), channel_id=1, source_target_pairs={{0,32},{16,48},{32,64},{48,80},{64,96},{80,112},{96,128},{112,144}... | collective-permute-start | bytes 196616 | tf_op jit(solution)/shard_map/ppermute | solution.py:12
  255.4 43.7 %collective-permute-start.4 = (f32[128,128]{0,1:T(8,128)S(1)}, f32[128,128]{0,1:T(8,128)S(1)}, u32[]{:S(2)}, u32[]{:S(2)}) collective-permute-start(f32[128,128]{0,1:T(8,128)S(1)} %fusion.4), channel_id=1, source_target_pairs={{0,32},{16,48},{32,64},{48,80},{64,96},{80,112},{96,128},{112,144}... | collective-permute-start | bytes 196616 | tf_op jit(solution)/shard_map/ppermute | solution.py:12
  258.7 42.1 %collective-permute-start.6 = (f32[128,128]{0,1:T(8,128)S(1)}, f32[128,128]{0,1:T(8,128)S(1)}, u32[]{:S(2)}, u32[]{:S(2)}) collective-permute-start(f32[128,128]{0,1:T(8,128)S(1)} %fusion.6), channel_id=1, source_target_pairs={{0,32},{16,48},{32,64},{48,80},{64,96},{80,112},{96,128},{112,144}... | collective-permute-start | bytes 196616 | tf_op jit(solution)/shard_map/ppermute | solution.py:12
  300.8 6.4 %collective-permute-start.5 = (f32[128,128]{0,1:T(8,128)S(1)}, f32[128,128]{0,1:T(8,128)S(1)}, u32[]{:S(2)}, u32[]{:S(2)}) collective-permute-start(f32[128,128]{0,1:T(8,128)S(1)} %get-tuple-element.239), channel_id=1, source_target_pairs={{0,64},{16,80},{32,96},{48,112},{64,128},{80,144},{96,160},{112,17... | collective-permute-start | bytes 196616 | tf_op jit(solution)/shard_map/ppermute | solution.py:12
  302.9 42.5 %collective-permute-start.7 = (f32[128,128]{0,1:T(8,128)S(1)}, f32[128,128]{0,1:T(8,128)S(1)}, u32[]{:S(2)}, u32[]{:S(2)}) collective-permute-start(f32[128,128]{0,1:T(8,128)S(1)} %fusion.3), channel_id=1, source_target_pairs={{0,64},{16,80},{32,96},{48,112},{64,128},{80,144},{96,160},{112,17... | collective-permute-start | bytes 196616 | tf_op jit(solution)/shard_map/ppermute | solution.py:12
  304.9 58.7 %collective-permute-start.9 = (f32[128,128]{0,1:T(8,128)S(1)}, f32[128,128]{0,1:T(8,128)S(1)}, u32[]{:S(2)}, u32[]{:S(2)}) collective-permute-start(f32[128,128]{0,1:T(8,128)S(1)} %get-tuple-element.238), channel_id=1, source_target_pairs={{0,64},{16,80},{32,96},{48,112},{64,128},{80,144},{96,160},{112,17... | collective-permute-start | bytes 196616 | tf_op jit(solution)/shard_map/ppermute | solution.py:12
  346.5 3.6 collective-permute-start.8
  348.0 40.3 %collective-permute-start.10 = (f32[128,128]{0,1:T(8,128)S(1)}, f32[128,128]{0,1:T(8,128)S(1)}, u32[]{:S(2)}, u32[]{:S(2)}) collective-permute-start(f32[128,128]{0,1:T(8,128)S(1)} %fusion.2), channel_id=1, source_target_pairs={{0,128},{16,144},{32,160},{48,176},{64,192},{80,208},{96,224},{112... | collective-permute-start | bytes 196616 | tf_op jit(solution)/shard_map/ppermute | solution.py:12
  389.3 13.0 %collective-permute-start.11 = (f32[128,128]{0,1:T(8,128)S(1)}, f32[128,128]{0,1:T(8,128)S(1)}, u32[]{:S(2)}, u32[]{:S(2)}) collective-permute-start(f32[128,128]{0,1:T(8,128)S(1)} %fusion), channel_id=1, source_target_pairs={{0,16},{16,32},{32,48},{48,64},{64,80},{80,96},{96,112},{112,128},... | collective-permute-start | bytes 196616 | tf_op jit(solution)/shard_map/ppermute | solution.py:12
  436.7 2.5 copy-start.3
  436.7 37.1 %copy-start.7 = (s32[1,16,2]{1,2,0:T(2,128)S(1)}, s32[1,16,2]{1,2,0:T(2,128)}, u32[]{:S(2)}) copy-start(s32[1,16,2]{1,2,0:T(2,128)} %param.58) | copy-start | bytes 388
  436.7 37.6 %copy-start.5 = (f32[1,1,4096]{2,1,0:T(1,128)S(1)}, f32[1,1,4096]{2,1,0:T(1,128)}, u32[]{:S(2)}) copy-start(f32[1,1,4096]{2,1,0:T(1,128)} %param.59) | copy-start | bytes 49156
  437.2 7.4 %collective-permute-start.12 = (f32[128,128]{1,0:T(8,128)S(1)}, f32[128,128]{1,0:T(8,128)S(1)}, u32[]{:S(2)}, u32[]{:S(2)}) collective-permute-start(f32[128,128]{1,0:T(8,128)S(1)} %fusion.218), channel_id=1, source_target_pairs={{16,0},{32,16},{48,32},{64,48},{80,64},{96,80},{112,96},{128,112},... | collective-permute-start | bytes 196616 | tf_op jit(solution)/shard_map/ppermute | solution.py:12
  439.6 7.5 %collective-permute-start.13 = (f32[128,128]{1,0:T(8,128)S(1)}, f32[128,128]{1,0:T(8,128)S(1)}, u32[]{:S(2)}, u32[]{:S(2)}) collective-permute-start(f32[128,128]{1,0:T(8,128)S(1)} %fusion.68), channel_id=1, source_target_pairs={{16,0},{32,16},{48,32},{64,48},{80,64},{96,80},{112,96},{128,112},... | collective-permute-start | bytes 196616 | tf_op jit(solution)/shard_map/ppermute | solution.py:12
  445.1 6.2 %collective-permute-start.14 = (f32[128,128]{0,1:T(8,128)S(1)}, f32[128,128]{0,1:T(8,128)S(1)}, u32[]{:S(2)}, u32[]{:S(2)}) collective-permute-start(f32[128,128]{0,1:T(8,128)S(1)} %convolution_add_fusion.5), channel_id=1, source_target_pairs={{32,0},{48,16},{64,32},{80,48},{96,64},{112,80},{128,96},{144,112}... | collective-permute-start | bytes 196616 | tf_op jit(solution)/shard_map/ppermute | solution.py:12
  447.3 6.6 %collective-permute-start.15 = (f32[128,128]{1,0:T(8,128)S(1)}, f32[128,128]{1,0:T(8,128)S(1)}, u32[]{:S(2)}, u32[]{:S(2)}) collective-permute-start(f32[128,128]{1,0:T(8,128)S(1)} %fusion.220), channel_id=1, source_target_pairs={{32,0},{48,16},{64,32},{80,48},{96,64},{112,80},{128,96},{144,112}... | collective-permute-start | bytes 196616 | tf_op jit(solution)/shard_map/ppermute | solution.py:12
  451.9 8.5 %collective-permute-start.16 = (f32[128,128]{0,1:T(8,128)S(1)}, f32[128,128]{0,1:T(8,128)S(1)}, u32[]{:S(2)}, u32[]{:S(2)}) collective-permute-start(f32[128,128]{0,1:T(8,128)S(1)} %convolution_add_fusion.4), channel_id=1, source_target_pairs={{64,0},{80,16},{96,32},{112,48},{128,64},{144,80},{160,96},{176,11... | collective-permute-start | bytes 196616 | tf_op jit(solution)/shard_map/ppermute | solution.py:12
  454.1 9.4 %collective-permute-start.17 = (f32[128,128]{1,0:T(8,128)S(1)}, f32[128,128]{1,0:T(8,128)S(1)}, u32[]{:S(2)}, u32[]{:S(2)}) collective-permute-start(f32[128,128]{1,0:T(8,128)S(1)} %fusion.222), channel_id=1, source_target_pairs={{64,0},{80,16},{96,32},{112,48},{128,64},{144,80},{160,96},{176,11... | collective-permute-start | bytes 196616 | tf_op jit(solution)/shard_map/ppermute | solution.py:12
  460.9 9.0 %collective-permute-start.18 = (f32[128,128]{0,1:T(8,128)S(1)}, f32[128,128]{0,1:T(8,128)S(1)}, u32[]{:S(2)}, u32[]{:S(2)}) collective-permute-start(f32[128,128]{0,1:T(8,128)S(1)} %convolution_add_fusion.3), channel_id=1, source_target_pairs={{128,0},{144,16},{160,32},{176,48},{192,64},{208,80},{224,96},{240... | collective-permute-start | bytes 196616 | tf_op jit(solution)/shard_map/ppermute | solution.py:12
  470.4 6.8 %collective-permute-start.19 = (f32[128,128]{0,1:T(8,128)S(1)}, f32[128,128]{0,1:T(8,128)S(1)}, u32[]{:S(2)}, u32[]{:S(2)}) collective-permute-start(f32[128,128]{0,1:T(8,128)S(1)} %convolution_add_fusion.2), channel_id=1, source_target_pairs={{16,0},{32,16},{48,32},{64,48},{80,64},{96,80},{112,96},{128,112},... | collective-permute-start | bytes 196616 | tf_op jit(solution)/shard_map/ppermute | solution.py:12
  492.4 10.7 %copy-start.6 = (s32[16,2]{0,1:T(2,128)S(1)}, s32[16,2]{0,1:T(2,128)}, u32[]{:S(2)}) copy-start(s32[16,2]{0,1:T(2,128)} %param.60) | copy-start | bytes 388
  496.4 15.0 %all-to-all-start = ((f32[1,16,4096]{2,0,1:T(1,128)}), f32[1,16,4096]{2,0,1:T(1,128)S(1)}, u32[]{:S(2)}, u32[]{:S(2)}) async-start(f32[1,16,4096]{2,0,1:T(1,128)} %reshape.651), calls=%async_computation | async-start | bytes 524288 | tf_op jit(solution)/shard_map/all_to_all | solution.py:146
where the time goes:
time: 527 us; the launch traced here: 518 us
  other arithmetic  316 us (60%)
  matrix products  70.4 us (13%)
  starting transfers between devices  61.9 us (12%)
  local copies, waits for them, and re-layouts  44.3 us (8%)
  waiting for transfers between devices  21.3 us (4%)
    another operation x21, other arithmetic, invert_small(): lower_factor = jnp.linalg.cholesky(matrix)  86.9 us
    another operation x14, other arithmetic, invert_small(): jax.scipy.linalg.solve_triangular(lower_factor, identity, lower=True)  73.4 us
    dot_general x74, matrix products, matmul(): return jnp.matmul(left_side, right_side, precision=lax.Precision.HIGHEST)  64.3 us
    ppermute x20, starting transfers between devices, passed_along(): lax.ppermute(value, axis, [(source, source + steps) for source in range(f...  55.2 us
    another operation x12, other arithmetic, combine(): root_reduced = jnp.linalg.cholesky(reduced)  49.6 us
    another operation x12, other arithmetic, combine(): root = jnp.linalg.cholesky(r_a)  49.6 us
    another operation x8, other arithmetic, lower_solve(): return jax.scipy.linalg.solve_triangular(lower_factor, rhs, lower=True)  41.9 us
    ppermute x20, waiting for transfers between devices, passed_along(): lax.ppermute(value, axis, [(source, source + steps) for source in range(f...  20 us
  transfers between devices with their start and end apart: 21, of which 9 were waited for; matrix products, arithmetic and copies ran while one was open for 33% of the time, Pallas kernels for 0%

commit v1 on v0

--- a/solution.py
+++ b/solution.py
@@ -66,8 +66,11 @@
 
 
 def self_energy(regrouped, derivative, pair_list):
-    first_pick = jnp.take(regrouped, pair_list[:, 0], axis=0)
-    second_pick = jnp.take(regrouped, pair_list[:, 1], axis=0)
+    energy_count = regrouped.shape[0]
+    flat = regrouped.reshape(energy_count, -1)
+    levels = jnp.arange(energy_count, dtype=pair_list.dtype)
+    first_pick = matmul((pair_list[:, 0:1] == levels).astype(flat.dtype), flat)
+    second_pick = matmul((pair_list[:, 1:2] == levels).astype(flat.dtype), flat)
     pair_count = pair_list.shape[0]
     listed = derivative.shape[0]
     first_pick = first_pick.reshape(pair_count, listed, BLK, BLK)
@@ -139,9 +142,13 @@
 
     local_density = jnp.diagonal(full)[None]
     block_count = size // BLK
-    picked = full.reshape(block_count, BLK, block_count, BLK)[
-        block_list[0, :, 0], :, block_list[0, :, 1], :
-    ]
+    row_blocks = full.reshape(block_count, BLK, size)[block_list[0, :, 0]]
+    orbital = jnp.arange(size, dtype=block_list.dtype)[None, :, None]
+    within = jnp.arange(BLK, dtype=block_list.dtype)[None, None, :]
+    column_pick = orbital == block_list[0, :, 1][:, None, None] * BLK + within
+    picked = jnp.einsum(
+        "bik,bkj->bij", row_blocks, column_pick.astype(full.dtype), precision=lax.Precision.HIGHEST
+    )
     picked = picked.reshape(1, block_list.shape[1], BLK * BLK)
     regrouped = lax.all_to_all(picked, "energy", split_axis=1, concat_axis=0, tiled=True)
     result = self_energy(regrouped, derivative[0], pair_list)

time: 527 us -> 528 us (level)
  local copies, waits for them, and re-layouts: 44.3 us -> 36.1 us
  matrix products: 70.4 us -> 75.9 us
    reshape x2 -> x0, local copies, waits for them, and re-layouts: 9.83 us -> none  [on_device(): full.reshape(block_count, BLK, block_count, BLK)]
    dot_general x74 -> x76, matrix products: 64.3 us -> 65.6 us  [matmul(): return jnp.matmul(left_side, right_side, precision=lax.Precision.HIGHEST)]
  transfers between devices with their start and end apart: 21 -> 21, of which waited for: 9 -> 8; matrix products, arithmetic and copies ran while one was open for 33% -> 33% of each run, Pallas kernels for 0% -> 0%
where the time goes in v1:
time: 528 us; the launch traced here: 518 us
  other arithmetic  316 us (60%)
  matrix products  75.9 us (14%)
  starting transfers between devices  64.6 us (12%)
  local copies, waits for them, and re-layouts  36.1 us (7%)
  waiting for transfers between devices  22 us (4%)
    another operation x21, other arithmetic, invert_small(): lower_factor = jnp.linalg.cholesky(matrix)  86.9 us
    another operation x14, other arithmetic, invert_small(): jax.scipy.linalg.solve_triangular(lower_factor, identity, lower=True)  73.4 us
    dot_general x76, matrix products, matmul(): return jnp.matmul(left_side, right_side, precision=lax.Precision.HIGHEST)  65.6 us
    ppermute x20, starting transfers between devices, passed_along(): lax.ppermute(value, axis, [(source, source + steps) for source in range(f...  57.6 us
    another operation x12, other arithmetic, combine(): root_reduced = jnp.linalg.cholesky(reduced)  49.6 us
    another operation x12, other arithmetic, combine(): root = jnp.linalg.cholesky(r_a)  49.6 us
    another operation x8, other arithmetic, lower_solve(): return jax.scipy.linalg.solve_triangular(lower_factor, rhs, lower=True)  41.9 us
    ppermute x20, waiting for transfers between devices, passed_along(): lax.ppermute(value, axis, [(source, source + steps) for source in range(f...  22 us
  transfers between devices with their start and end apart: 21, of which 8 were waited for; matrix products, arithmetic and copies ran while one was open for 33% of the time, Pallas kernels for 0%

profile of v1, /device:TPU:97, one launch (start us, length us, event | category | flops | bytes accessed | tf_op | source)
XLA Modules:
  0.0 518.5 jit_solution(1680301609628634664)
XLA Ops:
  9.8 11.7 %cholesky.239 = f32[128,128]{1,0:T(8,128)S(1)} custom-call(f32[128,128]{1,0:T(8,128)S(1)} %fusion.112), custom_call_target="Cholesky" | custom-call | tf_op jit(solution)/shard_map/jit(cholesky)/cholesky | solution.py:24
  22.8 9.8 %custom-call.19 = f32[1,128,128]{1,2,0:T(8,128)S(1)} custom-call(f32[1,128,128]{2,1,0:T(8,128)S(1)} %fusion.66), custom_call_target="InvertDiagBlocksLowerTriangular" | custom-call | tf_op jit(solution)/shard_map/jit(_solve_triangular)/triangular_solve | solution.py:26
  35.0 3.9 convolution_subtract_fusion.5
  43.8 11.7 %cholesky.250 = f32[128,128]{1,0:T(8,128)S(1)} custom-call(f32[128,128]{1,0:T(8,128)S(1)} %fusion.110), custom_call_target="Cholesky" | custom-call | tf_op jit(solution)/shard_map/jit(cholesky)/cholesky | solution.py:24
  56.9 9.8 %custom-call.20 = f32[1,128,128]{1,2,0:T(8,128)S(1)} custom-call(f32[1,128,128]{2,1,0:T(8,128)S(1)} %fusion.67), custom_call_target="InvertDiagBlocksLowerTriangular" | custom-call | tf_op jit(solution)/shard_map/jit(_solve_triangular)/triangular_solve | solution.py:26
  69.1 3.9 convolution_subtract_fusion.4
  77.4 11.9 %cholesky.261 = f32[128,128]{1,0:T(8,128)S(1)} custom-call(f32[128,128]{1,0:T(8,128)S(1)} %fusion.108), custom_call_target="Cholesky" | custom-call | tf_op jit(solution)/shard_map/jit(cholesky)/cholesky | solution.py:24
  90.6 9.8 %custom-call.21 = f32[1,128,128]{1,2,0:T(8,128)S(1)} custom-call(f32[1,128,128]{2,1,0:T(8,128)S(1)} %fusion.68), custom_call_target="InvertDiagBlocksLowerTriangular" | custom-call | tf_op jit(solution)/shard_map/jit(_solve_triangular)/triangular_solve | solution.py:26
  109.8 11.7 %cholesky.272 = f32[128,128]{1,0:T(8,128)S(1)} custom-call(f32[128,128]{1,0:T(8,128)S(1)} %fusion.106), custom_call_target="Cholesky" | custom-call | tf_op jit(solution)/shard_map/jit(cholesky)/cholesky | solution.py:24
  122.8 10.0 %custom-call.22 = f32[1,128,128]{1,2,0:T(8,128)S(1)} custom-call(f32[1,128,128]{2,1,0:T(8,128)S(1)} %fusion.69), custom_call_target="InvertDiagBlocksLowerTriangular" | custom-call | tf_op jit(solution)/shard_map/jit(_solve_triangular)/triangular_solve | solution.py:26
  135.2 3.9 convolution_subtract_fusion.2
  143.5 11.7 %cholesky.283 = f32[128,128]{1,0:T(8,128)S(1)} custom-call(f32[128,128]{1,0:T(8,128)S(1)} %fusion.104), custom_call_target="Cholesky" | custom-call | tf_op jit(solution)/shard_map/jit(cholesky)/cholesky | solution.py:24
  156.5 9.8 %custom-call.23 = f32[1,128,128]{1,2,0:T(8,128)S(1)} custom-call(f32[1,128,128]{2,1,0:T(8,128)S(1)} %fusion.70), custom_call_target="InvertDiagBlocksLowerTriangular" | custom-call | tf_op jit(solution)/shard_map/jit(_solve_triangular)/triangular_solve | solution.py:26
  168.1 3.5 convolution_subtract_fusion.1
  175.2 11.7 %cholesky.294 = f32[128,128]{1,0:T(8,128)S(1)} custom-call(f32[128,128]{1,0:T(8,128)S(1)} %fusion.102), custom_call_target="Cholesky" | custom-call | tf_op jit(solution)/shard_map/jit(cholesky)/cholesky | solution.py:24
  188.3 9.8 %custom-call.24 = f32[1,128,128]{1,2,0:T(8,128)S(1)} custom-call(f32[1,128,128]{2,1,0:T(8,128)S(1)} %fusion.71), custom_call_target="InvertDiagBlocksLowerTriangular" | custom-call | tf_op jit(solution)/shard_map/jit(_solve_triangular)/triangular_solve | solution.py:26
  199.3 5.3 %collective-permute-start.3 = (f32[128,128]{0,1:T(8,128)S(1)}, f32[128,128]{0,1:T(8,128)S(1)}, u32[]{:S(2)}, u32[]{:S(2)}) collective-permute-start(f32[128,128]{0,1:T(8,128)S(1)} %copy.234), channel_id=1, source_target_pairs={{0,16},{16,32},{32,48},{48,64},{64,80},{80,96},{96,112},{112,128},... | collective-permute-start | bytes 196616 | tf_op jit(solution)/shard_map/ppermute | solution.py:12
  210.1 3.2 collective-permute-start
  214.6 11.7 %cholesky.305 = f32[128,128]{1,0:T(8,128)S(1)} custom-call(f32[128,128]{1,0:T(8,128)S(1)} %fusion.100), custom_call_target="Cholesky" | custom-call | tf_op jit(solution)/shard_map/jit(cholesky)/cholesky | solution.py:54
  229.8 11.7 %cholesky.316 = f32[128,128]{1,0:T(8,128)S(1)} custom-call(f32[128,128]{1,0:T(8,128)S(1)} %fusion.99), custom_call_target="Cholesky" | custom-call | tf_op jit(solution)/shard_map/jit(cholesky)/cholesky | solution.py:58
  242.9 9.8 %custom-call.25 = f32[1,128,128]{1,2,0:T(8,128)S(1)} custom-call(f32[1,128,128]{2,1,0:T(8,128)S(1)} %fusion.72), custom_call_target="InvertDiagBlocksLowerTriangular" | custom-call | tf_op jit(solution)/shard_map/jit(_solve_triangular)/triangular_solve | solution.py:39
  253.7 2.6 collective-permute-start.2
  256.6 2.6 collective-permute-start.4
  262.2 11.7 %cholesky.327 = f32[128,128]{1,0:T(8,128)S(1)} custom-call(f32[128,128]{1,0:T(8,128)S(1)} %fusion.97), custom_call_target="Cholesky" | custom-call | tf_op jit(solution)/shard_map/jit(cholesky)/cholesky | solution.py:54
  277.4 11.7 %cholesky.338 = f32[128,128]{1,0:T(8,128)S(1)} custom-call(f32[128,128]{1,0:T(8,128)S(1)} %fusion.96), custom_call_target="Cholesky" | custom-call | tf_op jit(solution)/shard_map/jit(cholesky)/cholesky | solution.py:58
  290.5 9.8 %custom-call.26 = f32[1,128,128]{1,2,0:T(8,128)S(1)} custom-call(f32[1,128,128]{2,1,0:T(8,128)S(1)} %fusion.73), custom_call_target="InvertDiagBlocksLowerTriangular" | custom-call | tf_op jit(solution)/shard_map/jit(_solve_triangular)/triangular_solve | solution.py:39
  306.0 2.3 collective-permute-start.9
  308.5 11.7 %cholesky.349 = f32[128,128]{1,0:T(8,128)S(1)} custom-call(f32[128,128]{1,0:T(8,128)S(1)} %fusion.94), custom_call_target="Cholesky" | custom-call | tf_op jit(solution)/shard_map/jit(cholesky)/cholesky | solution.py:54
  323.8 11.7 %cholesky.360 = f32[128,128]{1,0:T(8,128)S(1)} custom-call(f32[128,128]{1,0:T(8,128)S(1)} %fusion.93), custom_call_target="Cholesky" | custom-call | tf_op jit(solution)/shard_map/jit(cholesky)/cholesky | solution.py:58
  336.8 9.8 %custom-call.27 = f32[1,128,128]{1,2,0:T(8,128)S(1)} custom-call(f32[1,128,128]{2,1,0:T(8,128)S(1)} %fusion.74), custom_call_target="InvertDiagBlocksLowerTriangular" | custom-call | tf_op jit(solution)/shard_map/jit(_solve_triangular)/triangular_solve | solution.py:39
  351.4 11.7 %cholesky.371 = f32[128,128]{1,0:T(8,128)S(1)} custom-call(f32[128,128]{1,0:T(8,128)S(1)} %fusion.91), custom_call_target="Cholesky" | custom-call | tf_op jit(solution)/shard_map/jit(cholesky)/cholesky | solution.py:54
  366.7 11.7 %cholesky.382 = f32[128,128]{1,0:T(8,128)S(1)} custom-call(f32[128,128]{1,0:T(8,128)S(1)} %fusion.90), custom_call_target="Cholesky" | custom-call | tf_op jit(solution)/shard_map/jit(cholesky)/cholesky | solution.py:58
  379.8 9.8 %custom-call.28 = f32[1,128,128]{1,2,0:T(8,128)S(1)} custom-call(f32[1,128,128]{2,1,0:T(8,128)S(1)} %fusion.75), custom_call_target="InvertDiagBlocksLowerTriangular" | custom-call | tf_op jit(solution)/shard_map/jit(_solve_triangular)/triangular_solve | solution.py:39
  390.5 14.3 %collective-permute-start.11 = (f32[128,128]{0,1:T(8,128)S(1)}, f32[128,128]{0,1:T(8,128)S(1)}, u32[]{:S(2)}, u32[]{:S(2)}) collective-permute-start(f32[128,128]{0,1:T(8,128)S(1)} %fusion.2), channel_id=1, source_target_pairs={{0,16},{16,32},{32,48},{48,64},{64,80},{80,96},{96,112},{112,128},... | collective-permute-start | bytes 196616 | tf_op jit(solution)/shard_map/ppermute | solution.py:12
  407.4 11.7 %cholesky.393 = f32[128,128]{1,0:T(8,128)S(1)} custom-call(f32[128,128]{1,0:T(8,128)S(1)} %fusion.88), custom_call_target="Cholesky" | custom-call | tf_op jit(solution)/shard_map/jit(cholesky)/cholesky | solution.py:24
  420.4 9.8 %custom-call.29 = f32[1,128,128]{1,2,0:T(8,128)S(1)} custom-call(f32[1,128,128]{2,1,0:T(8,128)S(1)} %fusion.76), custom_call_target="InvertDiagBlocksLowerTriangular" | custom-call | tf_op jit(solution)/shard_map/jit(_solve_triangular)/triangular_solve | solution.py:26
  432.6 3.9 convolution_subtract_fusion
  445.0 3.2 collective-permute-done.12
  457.6 2.2 collective-permute-start.17
  459.8 3.8 collective-permute-done.16
  467.3 5.8 %collective-permute-done.18 = f32[128,128]{0,1:T(8,128)S(1)} collective-permute-done((f32[128,128]{0,1:T(8,128)S(1)}, f32[128,128]{0,1:T(8,128)S(1)}, u32[]{:S(2)}, u32[]{:S(2)}) %collective-permute-start.18) | collective-permute-done | bytes 65568 | tf_op jit(solution)/shard_map/ppermute | solution.py:12
  473.6 3.5 collective-permute-start.19
  477.1 3.3 collective-permute-done.19
  481.9 3.9 convolution_add_fusion
  487.8 4.1 gather_fusion.1
  491.9 4.0 fusion
  496.9 7.0 %all-to-all-start = ((f32[1,16,4096]{2,0,1:T(1,128)}), f32[1,16,4096]{2,0,1:T(1,128)S(1)}, u32[]{:S(2)}, u32[]{:S(2)}) async-start(f32[1,16,4096]{2,0,1:T(1,128)} %reshape.607), calls=%async_computation | async-start | bytes 524288 | tf_op jit(solution)/shard_map/all_to_all | solution.py:153
  505.3 6.3 %gather_fusion = f32[768]{0:T(1024)S(1)} fusion(f32[768,768]{0,1:T(8,128)S(1)} %convolution_add_fusion, s32[768]{0:T(1024)S(1)} %or_reduce_fusion), kind=kCustom, calls=%fused_computation | custom fusion | bytes 12288 | tf_op jit(solution)/shard_map/jit(diagonal)/cond/branch_0_fun/gather | solution.py:143
  (280 shorter events, 134.7 us)
Async XLA Ops:
  0.6 5.4 %copy-start = (f32[1,128,128]{2,1,0:T(8,128)S(1)}, f32[1,128,128]{2,1,0:T(8,128)}, u32[]{:S(2)}) copy-start(f32[1,128,128]{2,1,0:T(8,128)} %param.55) | copy-start | bytes 196612
  4.4 1.6 copy-start.4
  43.7 23.3 %copy-start.1 = (f32[768,768]{0,1:T(8,128)}, f32[768,768]{0,1:T(8,128)S(1)}, u32[]{:S(2)}) copy-start(f32[768,768]{0,1:T(8,128)S(1)} %bitcast_dynamic-update-slice_fusion.4) | copy-start | bytes 7077892
  103.8 1.4 copy-start.2
  171.6 41.7 %copy-start.7 = (s32[1,16,2]{1,2,0:T(2,128)S(1)}, s32[1,16,2]{1,2,0:T(2,128)}, u32[]{:S(2)}) copy-start(s32[1,16,2]{1,2,0:T(2,128)} %param.56) | copy-start | bytes 388
  199.3 60.3 %collective-permute-start.3 = (f32[128,128]{0,1:T(8,128)S(1)}, f32[128,128]{0,1:T(8,128)S(1)}, u32[]{:S(2)}, u32[]{:S(2)}) collective-permute-start(f32[128,128]{0,1:T(8,128)S(1)} %copy.234), channel_id=1, source_target_pairs={{0,16},{16,32},{32,48},{48,64},{64,80},{80,96},{96,112},{112,128},... | collective-permute-start | bytes 196616 | tf_op jit(solution)/shard_map/ppermute | solution.py:12
  206.0 46.7 %collective-permute-start.1 = (f32[128,128]{0,1:T(8,128)S(1)}, f32[128,128]{0,1:T(8,128)S(1)}, u32[]{:S(2)}, u32[]{:S(2)}) collective-permute-start(f32[128,128]{0,1:T(8,128)S(1)} %convolution_negate_fusion), channel_id=1, source_target_pairs={{0,16},{16,32},{32,48},{48,64},{64,80},{80,96},{96,112},{112,128},... | collective-permute-start | bytes 196616 | tf_op jit(solution)/shard_map/ppermute | solution.py:12
  210.1 4.3 collective-permute-start
  253.7 8.3 %collective-permute-start.2 = (f32[128,128]{0,1:T(8,128)S(1)}, f32[128,128]{0,1:T(8,128)S(1)}, u32[]{:S(2)}, u32[]{:S(2)}) collective-permute-start(f32[128,128]{0,1:T(8,128)S(1)} %add_select_fusion.2), channel_id=1, source_target_pairs={{0,32},{16,48},{32,64},{48,80},{64,96},{80,112},{96,128},{112,144}... | collective-permute-start | bytes 196616 | tf_op jit(solution)/shard_map/ppermute | solution.py:12
  256.6 43.7 %collective-permute-start.4 = (f32[128,128]{0,1:T(8,128)S(1)}, f32[128,128]{0,1:T(8,128)S(1)}, u32[]{:S(2)}, u32[]{:S(2)}) collective-permute-start(f32[128,128]{0,1:T(8,128)S(1)} %fusion.6), channel_id=1, source_target_pairs={{0,32},{16,48},{32,64},{48,80},{64,96},{80,112},{96,128},{112,144}... | collective-permute-start | bytes 196616 | tf_op jit(solution)/shard_map/ppermute | solution.py:12
  259.9 42.1 %collective-permute-start.6 = (f32[128,128]{0,1:T(8,128)S(1)}, f32[128,128]{0,1:T(8,128)S(1)}, u32[]{:S(2)}, u32[]{:S(2)}) collective-permute-start(f32[128,128]{0,1:T(8,128)S(1)} %fusion.8), channel_id=1, source_target_pairs={{0,32},{16,48},{32,64},{48,80},{64,96},{80,112},{96,128},{112,144}... | collective-permute-start | bytes 196616 | tf_op jit(solution)/shard_map/ppermute | solution.py:12
  302.0 6.4 %collective-permute-start.5 = (f32[128,128]{0,1:T(8,128)S(1)}, f32[128,128]{0,1:T(8,128)S(1)}, u32[]{:S(2)}, u32[]{:S(2)}) collective-permute-start(f32[128,128]{0,1:T(8,128)S(1)} %get-tuple-element.234), channel_id=1, source_target_pairs={{0,64},{16,80},{32,96},{48,112},{64,128},{80,144},{96,160},{112,17... | collective-permute-start | bytes 196616 | tf_op jit(solution)/shard_map/ppermute | solution.py:12
  304.1 42.5 %collective-permute-start.7 = (f32[128,128]{0,1:T(8,128)S(1)}, f32[128,128]{0,1:T(8,128)S(1)}, u32[]{:S(2)}, u32[]{:S(2)}) collective-permute-start(f32[128,128]{0,1:T(8,128)S(1)} %fusion.5), channel_id=1, source_target_pairs={{0,64},{16,80},{32,96},{48,112},{64,128},{80,144},{96,160},{112,17... | collective-permute-start | bytes 196616 | tf_op jit(solution)/shard_map/ppermute | solution.py:12
  306.0 58.7 %collective-permute-start.9 = (f32[128,128]{0,1:T(8,128)S(1)}, f32[128,128]{0,1:T(8,128)S(1)}, u32[]{:S(2)}, u32[]{:S(2)}) collective-permute-start(f32[128,128]{0,1:T(8,128)S(1)} %get-tuple-element.233), channel_id=1, source_target_pairs={{0,64},{16,80},{32,96},{48,112},{64,128},{80,144},{96,160},{112,17... | collective-permute-start | bytes 196616 | tf_op jit(solution)/shard_map/ppermute | solution.py:12
  347.7 3.6 collective-permute-start.8
  349.2 40.3 %collective-permute-start.10 = (f32[128,128]{0,1:T(8,128)S(1)}, f32[128,128]{0,1:T(8,128)S(1)}, u32[]{:S(2)}, u32[]{:S(2)}) collective-permute-start(f32[128,128]{0,1:T(8,128)S(1)} %fusion.4), channel_id=1, source_target_pairs={{0,128},{16,144},{32,160},{48,176},{64,192},{80,208},{96,224},{112... | collective-permute-start | bytes 196616 | tf_op jit(solution)/shard_map/ppermute | solution.py:12
  390.5 15.4 %collective-permute-start.11 = (f32[128,128]{0,1:T(8,128)S(1)}, f32[128,128]{0,1:T(8,128)S(1)}, u32[]{:S(2)}, u32[]{:S(2)}) collective-permute-start(f32[128,128]{0,1:T(8,128)S(1)} %fusion.2), channel_id=1, source_target_pairs={{0,16},{16,32},{32,48},{48,64},{64,80},{80,96},{96,112},{112,128},... | collective-permute-start | bytes 196616 | tf_op jit(solution)/shard_map/ppermute | solution.py:12
  440.3 2.4 copy-start.3
  440.8 7.4 %collective-permute-start.12 = (f32[128,128]{1,0:T(8,128)S(1)}, f32[128,128]{1,0:T(8,128)S(1)}, u32[]{:S(2)}, u32[]{:S(2)}) collective-permute-start(f32[128,128]{1,0:T(8,128)S(1)} %fusion.228), channel_id=1, source_target_pairs={{16,0},{32,16},{48,32},{64,48},{80,64},{96,80},{112,96},{128,112},... | collective-permute-start | bytes 196616 | tf_op jit(solution)/shard_map/ppermute | solution.py:12
  443.1 7.5 %collective-permute-start.13 = (f32[128,128]{1,0:T(8,128)S(1)}, f32[128,128]{1,0:T(8,128)S(1)}, u32[]{:S(2)}, u32[]{:S(2)}) collective-permute-start(f32[128,128]{1,0:T(8,128)S(1)} %fusion.77), channel_id=1, source_target_pairs={{16,0},{32,16},{48,32},{64,48},{80,64},{96,80},{112,96},{128,112},... | collective-permute-start | bytes 196616 | tf_op jit(solution)/shard_map/ppermute | solution.py:12
  448.7 6.2 %collective-permute-start.14 = (f32[128,128]{0,1:T(8,128)S(1)}, f32[128,128]{0,1:T(8,128)S(1)}, u32[]{:S(2)}, u32[]{:S(2)}) collective-permute-start(f32[128,128]{0,1:T(8,128)S(1)} %convolution_add_fusion.5), channel_id=1, source_target_pairs={{32,0},{48,16},{64,32},{80,48},{96,64},{112,80},{128,96},{144,112}... | collective-permute-start | bytes 196616 | tf_op jit(solution)/shard_map/ppermute | solution.py:12
  450.8 6.5 %collective-permute-start.15 = (f32[128,128]{1,0:T(8,128)S(1)}, f32[128,128]{1,0:T(8,128)S(1)}, u32[]{:S(2)}, u32[]{:S(2)}) collective-permute-start(f32[128,128]{1,0:T(8,128)S(1)} %fusion.230), channel_id=1, source_target_pairs={{32,0},{48,16},{64,32},{80,48},{96,64},{112,80},{128,96},{144,112}... | collective-permute-start | bytes 196616 | tf_op jit(solution)/shard_map/ppermute | solution.py:12
  455.4 8.2 %collective-permute-start.16 = (f32[128,128]{0,1:T(8,128)S(1)}, f32[128,128]{0,1:T(8,128)S(1)}, u32[]{:S(2)}, u32[]{:S(2)}) collective-permute-start(f32[128,128]{0,1:T(8,128)S(1)} %convolution_add_fusion.4), channel_id=1, source_target_pairs={{64,0},{80,16},{96,32},{112,48},{128,64},{144,80},{160,96},{176,11... | collective-permute-start | bytes 196616 | tf_op jit(solution)/shard_map/ppermute | solution.py:12
  457.6 9.5 %collective-permute-start.17 = (f32[128,128]{1,0:T(8,128)S(1)}, f32[128,128]{1,0:T(8,128)S(1)}, u32[]{:S(2)}, u32[]{:S(2)}) collective-permute-start(f32[128,128]{1,0:T(8,128)S(1)} %fusion.232), channel_id=1, source_target_pairs={{64,0},{80,16},{96,32},{112,48},{128,64},{144,80},{160,96},{176,11... | collective-permute-start | bytes 196616 | tf_op jit(solution)/shard_map/ppermute | solution.py:12
  464.1 8.9 %collective-permute-start.18 = (f32[128,128]{0,1:T(8,128)S(1)}, f32[128,128]{0,1:T(8,128)S(1)}, u32[]{:S(2)}, u32[]{:S(2)}) collective-permute-start(f32[128,128]{0,1:T(8,128)S(1)} %convolution_add_fusion.3), channel_id=1, source_target_pairs={{128,0},{144,16},{160,32},{176,48},{192,64},{208,80},{224,96},{240... | collective-permute-start | bytes 196616 | tf_op jit(solution)/shard_map/ppermute | solution.py:12
  473.6 6.8 %collective-permute-start.19 = (f32[128,128]{0,1:T(8,128)S(1)}, f32[128,128]{0,1:T(8,128)S(1)}, u32[]{:S(2)}, u32[]{:S(2)}) collective-permute-start(f32[128,128]{0,1:T(8,128)S(1)} %convolution_add_fusion.2), channel_id=1, source_target_pairs={{16,0},{32,16},{48,32},{64,48},{80,64},{96,80},{112,96},{128,112},... | collective-permute-start | bytes 196616 | tf_op jit(solution)/shard_map/ppermute | solution.py:12
  491.9 12.6 %copy-start.5 = (f32[1,1,4096]{2,1,0:T(1,128)S(1)}, f32[1,1,4096]{2,1,0:T(1,128)}, u32[]{:S(2)}) copy-start(f32[1,1,4096]{2,1,0:T(1,128)} %param.57) | copy-start | bytes 49156
  491.9 13.4 %copy-start.6 = (s32[16,2]{0,1:T(2,128)S(1)}, s32[16,2]{0,1:T(2,128)}, u32[]{:S(2)}) copy-start(s32[16,2]{0,1:T(2,128)} %param.58) | copy-start | bytes 388
  496.9 15.3 %all-to-all-start = ((f32[1,16,4096]{2,0,1:T(1,128)}), f32[1,16,4096]{2,0,1:T(1,128)S(1)}, u32[]{:S(2)}, u32[]{:S(2)}) async-start(f32[1,16,4096]{2,0,1:T(1,128)} %reshape.607), calls=%async_computation | async-start | bytes 524288 | tf_op jit(solution)/shard_map/all_to_all | solution.py:153
